TPU v7x, 128 devices: a whole 4x4x4 slice. The times are simulated.
128 devices in a mesh: expert: 4 (over z_lo, core), fsdp: 32 (over y, z_hi, x).
Axes of the slice: x: 4, y: 4, z: 4 (z_hi: 2, z_lo: 2; z = z_hi * 2 + z_lo), core: 2. Of those that a mesh axis runs over, the one named last changes fastest.
Arguments:
- tokens: bfloat16 [16384, 2048], P(('expert', 'fsdp')), may hold values from -6 to 6
- expert_ids: int32 [16384, 1], P(('expert', 'fsdp')), may hold values from 0 to 7; in each aligned block of 128 rows (0 to 127, 128 to 255, ...) at most 24 rows name the same one
- gate_weight: bfloat16 [8, 2048, 8192], P('expert', None, 'fsdp'), may hold values from -0.125 to 0.125
- up_weight: bfloat16 [8, 2048, 8192], P('expert', None, 'fsdp'), may hold values from -0.125 to 0.125
- hidden_grad: bfloat16 [8, 3072, 8192], P('expert', None, 'fsdp'), may hold values from -0.1796875 to 0.1796875
Outputs:
- hidden: bfloat16 [8, 3072, 8192], P('expert', None, 'fsdp')
- gate_grad: float32 [8, 2048, 8192], P('expert', None, 'fsdp')
- up_grad: float32 [8, 2048, 8192], P('expert', None, 'fsdp')
Inputs may be any that keep to these rules, and one draw needn't show every extreme that they name: `expert_ids`: within the tokens of one device (aligned blocks of 128 rows) no expert is named more than 24 times, a bound that some block reaches.
All inputs are finite; a program needn't handle non-finite values.
Results may differ from a plain program's by a relative error of at most 0.003.
Values may be sent and summed in bfloat16 or wider, within the bound.
No kernel may reach another device: no remote copies, remote signals or barrier semaphores. Data moves between devices by JAX's collectives and lax.ppermute only.
A program may use at most 192 MiB of HBM per device.

v0:
```python
import jax
import jax.numpy as jnp
from jax import lax
from jax.sharding import PartitionSpec as P

CAP = 24


def chunk_pass(rows, gate_w, up_w, cotan):
    gate = jnp.einsum("grd,gdf->grf", rows, gate_w, preferred_element_type=jnp.float32)
    upval = jnp.einsum("grd,gdf->grf", rows, up_w, preferred_element_type=jnp.float32)
    cotan = cotan.astype(jnp.float32)
    sigma = 1.0 / (1.0 + jnp.exp(-gate))
    active = gate * sigma
    hidden = (active * upval).astype(jnp.bfloat16)
    gate_delta = (cotan * upval * sigma * (1.0 + gate * (1.0 - sigma))).astype(jnp.bfloat16)
    up_delta = (cotan * active).astype(jnp.bfloat16)
    gate_sum = jnp.einsum("grd,grf->gdf", rows, gate_delta, preferred_element_type=jnp.float32)
    up_sum = jnp.einsum("grd,grf->gdf", rows, up_delta, preferred_element_type=jnp.float32)
    return (hidden, gate_sum, up_sum)


def on_device(tokens, expert_ids, gate_weight, up_weight, hidden_grad):
    owners = lax.axis_size("expert")
    members = lax.axis_size("fsdp")
    per_owner = gate_weight.shape[0]
    model = gate_weight.shape[1]
    route = expert_ids[:, 0]
    total_experts = per_owner * owners
    onehot = (route[:, None] == jnp.arange(total_experts, dtype=jnp.int32)[None, :]).astype(
        jnp.int32
    )
    rank = jnp.sum((jnp.cumsum(onehot, axis=0) - onehot) * onehot, axis=1)
    owner_of = route // per_owner
    within = route % per_owner
    target = owner_of * (per_owner * CAP) + within * CAP + rank
    send_rows = per_owner * owners * CAP
    placing = (jnp.arange(send_rows, dtype=jnp.int32)[:, None] == target[None, :]).astype(
        jnp.bfloat16
    )
    outgoing = jnp.dot(placing, tokens, preferred_element_type=jnp.float32).astype(jnp.bfloat16)
    outgoing = outgoing.reshape(owners, per_owner, CAP, model)
    arrived = lax.all_to_all(outgoing, "expert", split_axis=0, concat_axis=0, tiled=True)
    slot_count = members * CAP

    def gather(source):
        piece = lax.dynamic_index_in_dim(arrived, source, axis=0, keepdims=False)
        return lax.all_gather(piece, "fsdp", axis=1, tiled=True)

    def step(source, rows, hidden_buf, gate_acc, up_acc):
        start = source * slot_count
        cotan = lax.dynamic_slice_in_dim(hidden_grad, start, slot_count, axis=1)
        hidden, gate_sum, up_sum = chunk_pass(rows, gate_weight, up_weight, cotan)
        hidden_buf = lax.dynamic_update_slice_in_dim(hidden_buf, hidden, start, axis=1)
        return (hidden_buf, gate_acc + gate_sum, up_acc + up_sum)

    def body(source, carry):
        rows, hidden_buf, gate_acc, up_acc = carry
        next_rows = gather(source + 1)
        hidden_buf, gate_acc, up_acc = step(source, rows, hidden_buf, gate_acc, up_acc)
        return (next_rows, hidden_buf, gate_acc, up_acc)

    hidden_buf = jnp.zeros(hidden_grad.shape, jnp.bfloat16)
    gate_acc = jnp.zeros(gate_weight.shape, jnp.float32)
    up_acc = jnp.zeros(up_weight.shape, jnp.float32)
    rows = gather(0)
    rows, hidden_buf, gate_acc, up_acc = lax.fori_loop(
        0, owners - 1, body, (rows, hidden_buf, gate_acc, up_acc)
    )
    hidden_buf, gate_acc, up_acc = step(owners - 1, rows, hidden_buf, gate_acc, up_acc)
    return (hidden_buf, gate_acc, up_acc)


def solution(mesh):
    in_specs = (
        P(("expert", "fsdp"), None),
        P(("expert", "fsdp"), None),
        P("expert", None, "fsdp"),
        P("expert", None, "fsdp"),
        P("expert", None, "fsdp"),
    )
    out_specs = (P("expert", None, "fsdp"), P("expert", None, "fsdp"), P("expert", None, "fsdp"))
    return jax.shard_map(
        on_device, mesh=mesh, in_specs=in_specs, out_specs=out_specs, check_vma=False
    )
```

profile of v0, /device:TPU:1, one launch (start us, length us, event | category | flops | bytes accessed | tf_op | source)
XLA Modules:
  0.0 467.2 jit_solution(2851810721346810936)
XLA Ops:
  7.2 0.8 fusion.28
  8.2 0.8 select_reduce_fusion
  10.1 15.1 %all_to_all.5 = bf16[4,2,24,2048]{3,2,1,0:T(8,128)(2,1)S(1)} all-to-all(bf16[4,2,24,2048]{3,2,1,0:T(8,128)(2,1)S(1)} %bitcast.46), channel_id=1, replica_groups=mesh['expert'=4,'fsdp'=32] {'expert'}, dimensions={0} | all-to-all | bytes 1572864 | tf_op jit(solution)/shard_map/all_to_all | solution.py:43
  25.9 94.5 %all-gather.8.cloned.1.call-done = bf16[1,2,768,2048]{3,2,1,0:T(8,128)(2,1)} async-done(((bf16[1,2,24,2048]{3,2,1,0:T(8,128)(2,1)}), bf16[1,2,768,2048]{3,2,1,0:T(8,128)(2,1)}) %all-gather.8.cloned.1.call-update) | async-done | bytes 6291472 | tf_op jit(solution)/shard_map/all_gather | solution.py:48
  120.4 1.9 broadcast_in_dim.2
  122.3 301.8 %while.22 = (s32[]{:T(128)}, bf16[2,768,2048]{2,1,0:T(8,128)(2,1)}, bf16[2,3072,256]{2,1,0:T(8,128)(2,1)}, f32[2,2048,256]{1,2,0:T(8,128)}, f32[2,2048,256]{1,2,...) while((s32[]{:T(128)}, bf16[2,768,2048]{2,1,0:T(8,128)(2,1)}, ...), condition=%wide.region_3.4_spmd.clone, body=%wide.region_2.3_spmd.clone.sunk | while | flops 6456082432 | bytes 130220424 | solution.py:67
  123.0 5.3 %fusion.68 = f32[2,768,256]{2,1,0:T(8,128)S(1)} fusion(bf16[2,768,2048]{2,1,0:T(8,128)(2,1)} %get-tuple-element.356, bf16[2,2048,256]{2,1,0:T(8,128)(2,1)} %get-tuple-element.375), kind=kOutput, calls=%fused_computation.51.clone.1 | convolution fusion | flops 1610612736 | bytes 9961472 | tf_op jit(solution)/shard_map/while/body/eval_jaxpr/grd,gdf->grf/dot_general | solution.py:10
  128.8 2.9 fusion.69
  131.8 4.1 bitcast_add_fusion.5
  135.9 4.4 bitcast_add_fusion.4
  140.3 76.2 %all-gather.10.cloned.1.call-done = bf16[1,2,768,2048]{3,2,1,0:T(8,128)(2,1)} async-done(((bf16[1,2,24,2048]{3,2,1,0:T(8,128)(2,1)}), bf16[1,2,768,2048]{3,2,1,0:T(8,128)(2,1)}) %all-gather.10.cloned.1.call-update) | async-done | bytes 6291472 | tf_op jit(solution)/shard_map/while/body/eval_jaxpr/all_gather | solution.py:48
  216.4 6.6 %copy.30 = bf16[2,768,2048]{2,1,0:T(8,128)(2,1)} copy(bf16[2,768,2048]{2,1,0:T(8,128)(2,1)} %bitcast.40) | data formatting | bytes 12582912 | tf_op jit(solution)/shard_map/while
  223.0 0.7 constant_dynamic-slice_fusion.2
  223.7 5.3 %fusion.68 = f32[2,768,256]{2,1,0:T(8,128)S(1)} fusion(bf16[2,768,2048]{2,1,0:T(8,128)(2,1)} %get-tuple-element.356, bf16[2,2048,256]{2,1,0:T(8,128)(2,1)} %get-tuple-element.375), kind=kOutput, calls=%fused_computation.51.clone.1 | convolution fusion | flops 1610612736 | bytes 9961472 | tf_op jit(solution)/shard_map/while/body/eval_jaxpr/grd,gdf->grf/dot_general | solution.py:10
  229.5 2.9 fusion.69
  232.5 6.3 %bitcast_add_fusion.5 = f32[2,2048,256]{1,2,0:T(8,128)} fusion(f32[2,2048,256]{1,2,0:T(8,128)} %get-tuple-element.359, bf16[2,768,2048]{2,1,0:T(8,128)(2,1)S(1)} %bitcast.43, pred[]{:T(512)S(6)} %compare.14, bf16[2,3072,256]{2,1,0:T(8,128)(2,1)S(1)} %copy-done.4, s32[]{:T(128)S(6)} %select_n.61, f32[2,768,256]{2,1,0:T(8,128)S(1)} %fusion.68), kind=kOutput, calls=%fused_computation.clone.1 | convolution fusion | flops 1615462400 | bytes 17039364 | tf_op jit(solution)/shard_map/while/body/eval_jaxpr/grd,grf->gdf/dot_general | solution.py:19
  238.8 6.6 %bitcast_add_fusion.4 = f32[2,2048,256]{1,2,0:T(8,128)} fusion(f32[2,2048,256]{1,2,0:T(8,128)} %get-tuple-element.358, bf16[2,768,2048]{2,1,0:T(8,128)(2,1)S(1)} %bitcast.43, pred[]{:T(512)S(6)} %compare.14, f32[2,768,256]{2,1,0:T(8,128)S(1)} %get-tuple-element.340, f32[2,768,256]{2,1,0:T(8,128)S(1)} %fusion.68, ...), kind=kOutput, calls=%fused_computation.1.clone.1 | convolution fusion | flops 1617035264 | bytes 18612228 | tf_op jit(solution)/shard_map/while/body/eval_jaxpr/grd,grf->gdf/dot_general | solution.py:18
  245.3 71.8 %all-gather.10.cloned.1.call-done = bf16[1,2,768,2048]{3,2,1,0:T(8,128)(2,1)} async-done(((bf16[1,2,24,2048]{3,2,1,0:T(8,128)(2,1)}), bf16[1,2,768,2048]{3,2,1,0:T(8,128)(2,1)}) %all-gather.10.cloned.1.call-update) | async-done | bytes 6291472 | tf_op jit(solution)/shard_map/while/body/eval_jaxpr/all_gather | solution.py:48
  317.1 6.6 %copy.30 = bf16[2,768,2048]{2,1,0:T(8,128)(2,1)} copy(bf16[2,768,2048]{2,1,0:T(8,128)(2,1)} %bitcast.40) | data formatting | bytes 12582912 | tf_op jit(solution)/shard_map/while
  323.7 0.7 constant_dynamic-slice_fusion.2
  324.4 5.3 %fusion.68 = f32[2,768,256]{2,1,0:T(8,128)S(1)} fusion(bf16[2,768,2048]{2,1,0:T(8,128)(2,1)} %get-tuple-element.356, bf16[2,2048,256]{2,1,0:T(8,128)(2,1)} %get-tuple-element.375), kind=kOutput, calls=%fused_computation.51.clone.1 | convolution fusion | flops 1610612736 | bytes 9961472 | tf_op jit(solution)/shard_map/while/body/eval_jaxpr/grd,gdf->grf/dot_general | solution.py:10
  330.2 2.9 fusion.69
  333.2 6.3 %bitcast_add_fusion.5 = f32[2,2048,256]{1,2,0:T(8,128)} fusion(f32[2,2048,256]{1,2,0:T(8,128)} %get-tuple-element.359, bf16[2,768,2048]{2,1,0:T(8,128)(2,1)S(1)} %bitcast.43, pred[]{:T(512)S(6)} %compare.14, bf16[2,3072,256]{2,1,0:T(8,128)(2,1)S(1)} %copy-done.4, s32[]{:T(128)S(6)} %select_n.61, f32[2,768,256]{2,1,0:T(8,128)S(1)} %fusion.68), kind=kOutput, calls=%fused_computation.clone.1 | convolution fusion | flops 1615462400 | bytes 17039364 | tf_op jit(solution)/shard_map/while/body/eval_jaxpr/grd,grf->gdf/dot_general | solution.py:19
  339.4 6.6 %bitcast_add_fusion.4 = f32[2,2048,256]{1,2,0:T(8,128)} fusion(f32[2,2048,256]{1,2,0:T(8,128)} %get-tuple-element.358, bf16[2,768,2048]{2,1,0:T(8,128)(2,1)S(1)} %bitcast.43, pred[]{:T(512)S(6)} %compare.14, f32[2,768,256]{2,1,0:T(8,128)S(1)} %get-tuple-element.340, f32[2,768,256]{2,1,0:T(8,128)S(1)} %fusion.68, ...), kind=kOutput, calls=%fused_computation.1.clone.1 | convolution fusion | flops 1617035264 | bytes 18612228 | tf_op jit(solution)/shard_map/while/body/eval_jaxpr/grd,grf->gdf/dot_general | solution.py:18
  346.0 71.5 %all-gather.10.cloned.1.call-done = bf16[1,2,768,2048]{3,2,1,0:T(8,128)(2,1)} async-done(((bf16[1,2,24,2048]{3,2,1,0:T(8,128)(2,1)}), bf16[1,2,768,2048]{3,2,1,0:T(8,128)(2,1)}) %all-gather.10.cloned.1.call-update) | async-done | bytes 6291472 | tf_op jit(solution)/shard_map/while/body/eval_jaxpr/all_gather | solution.py:48
  417.5 6.6 %copy.30 = bf16[2,768,2048]{2,1,0:T(8,128)(2,1)} copy(bf16[2,768,2048]{2,1,0:T(8,128)(2,1)} %bitcast.40) | data formatting | bytes 12582912 | tf_op jit(solution)/shard_map/while
  424.1 5.5 %copy.13 = f32[2,2048,256]{2,1,0:T(8,128)} copy(f32[2,2048,256]{1,2,0:T(8,128)} %get-tuple-element.229) | data formatting | bytes 8388608 | tf_op jit(solution)/shard_map/while | solution.py:67
  429.6 5.3 %fusion.36 = f32[2,768,256]{2,1,0:T(8,128)S(1)} fusion(bf16[2,768,2048]{2,1,0:T(8,128)(2,1)} %get-tuple-element.227, bf16[2,2048,256]{2,1,0:T(8,128)(2,1)} %get-tuple-element.392), kind=kOutput, calls=%fused_computation.52 | convolution fusion | flops 1610612736 | bytes 9961472 | tf_op jit(solution)/shard_map/grd,gdf->grf/dot_general | solution.py:10
  435.5 6.7 %convolution_add_fusion = f32[2,2048,256]{2,1,0:T(8,128)} fusion(f32[2,2048,256]{2,1,0:T(8,128)S(1)} %copy-done.1, bf16[2,768,2048]{2,1,0:T(8,128)(2,1)S(1)} %bitcast.45, bf16[2,3072,256]{2,1,0:T(8,128)(2,1)} %get-tuple-element.389, f32[2,768,256]{2,1,0:T(8,128)S(1)} %fusion.36), kind=kOutput, calls=%fused_computation.20 | convolution fusion | flops 1614413824 | bytes 17039360 | tf_op jit(solution)/shard_map/grd,grf->gdf/dot_general | solution.py:19
  442.2 3.4 fusion.21
  445.6 5.5 %copy.11 = f32[2,2048,256]{2,1,0:T(8,128)} copy(f32[2,2048,256]{1,2,0:T(8,128)} %get-tuple-element.228) | data formatting | bytes 8388608 | tf_op jit(solution)/shard_map/while | solution.py:67
  451.1 9.6 %convolution_add_fusion.1 = f32[2,2048,256]{2,1,0:T(8,128)} fusion(f32[2,2048,256]{2,1,0:T(8,128)} %copy.11, bf16[2,768,2048]{2,1,0:T(8,128)(2,1)} %get-tuple-element.227, f32[2,768,256]{2,1,0:T(8,128)} %get-tuple-element.281, f32[2,768,256]{2,1,0:T(8,128)S(1)} %copy-done.3, bf16[2,3072,256]{2,1,0:T(8,128)(2,1)} %get-tuple-element.389), kind=kOutput, calls=%fused_computation.21 | convolution fusion | flops 1615986688 | bytes 18612224 | tf_op jit(solution)/shard_map/grd,grf->gdf/dot_general | solution.py:18
  (57 shorter events, 4.6 us)
Async XLA Ops:
  7.2 2.5 copy-start
  7.2 113.2 %all-gather.8.cloned.1.call-start = ((), (), s32[]{:S(2)}) async-start(), calls=%async_computation.1 | async-start | bytes 6488064 | tf_op jit(solution)/shard_map/all_gather | solution.py:48
  122.3 94.1 %all-gather.10.cloned.1.call-start = ((), (), s32[]{:S(2)}) async-start(), calls=%async_computation.2 | async-start | bytes 6488064 | tf_op jit(solution)/shard_map/while/body/eval_jaxpr/all_gather | solution.py:48
  123.0 5.4 %slice-start = ((s8[6291456]{0:T(1024)(128)(4,1)}), s8[2097152]{0:T(1024)(128)(4,1)S(1)}, s32[]{:S(2)}) async-start(s8[6291456]{0:T(1024)(128)(4,1)} %bitcast.42), calls=%async_computation.3 | async-start | bytes 4194304 | tf_op jit(solution)/shard_map/while
  123.0 5.4 %slice-start.1 = ((s8[6291456]{0:T(1024)(128)(4,1)}), s8[4194304]{0:T(1024)(128)(4,1)S(1)}, s32[]{:S(2)}) async-start(s8[6291456]{0:T(1024)(128)(4,1)} %bitcast.42), calls=%async_computation.4 | async-start | bytes 8388608 | tf_op jit(solution)/shard_map/while
  123.0 5.8 %copy-start.5 = (bf16[2,2048,256]{2,1,0:T(8,128)(2,1)S(1)}, bf16[2,2048,256]{2,1,0:T(8,128)(2,1)}, u32[]{:S(2)}) copy-start(bf16[2,2048,256]{2,1,0:T(8,128)(2,1)} %get-tuple-element.376) | copy-start | bytes 6291460 | tf_op jit(solution)/shard_map/while
  128.8 2.9 copy-start.4
  223.0 94.1 %all-gather.10.cloned.1.call-start = ((), (), s32[]{:S(2)}) async-start(), calls=%async_computation.2 | async-start | bytes 6488064 | tf_op jit(solution)/shard_map/while/body/eval_jaxpr/all_gather | solution.py:48
  223.7 5.4 %slice-start = ((s8[6291456]{0:T(1024)(128)(4,1)}), s8[2097152]{0:T(1024)(128)(4,1)S(1)}, s32[]{:S(2)}) async-start(s8[6291456]{0:T(1024)(128)(4,1)} %bitcast.42), calls=%async_computation.3 | async-start | bytes 4194304 | tf_op jit(solution)/shard_map/while
  223.7 5.4 %slice-start.1 = ((s8[6291456]{0:T(1024)(128)(4,1)}), s8[4194304]{0:T(1024)(128)(4,1)S(1)}, s32[]{:S(2)}) async-start(s8[6291456]{0:T(1024)(128)(4,1)} %bitcast.42), calls=%async_computation.4 | async-start | bytes 8388608 | tf_op jit(solution)/shard_map/while
  223.7 5.8 %copy-start.5 = (bf16[2,2048,256]{2,1,0:T(8,128)(2,1)S(1)}, bf16[2,2048,256]{2,1,0:T(8,128)(2,1)}, u32[]{:S(2)}) copy-start(bf16[2,2048,256]{2,1,0:T(8,128)(2,1)} %get-tuple-element.376) | copy-start | bytes 6291460 | tf_op jit(solution)/shard_map/while
  229.5 2.9 copy-start.4
  323.7 93.8 %all-gather.10.cloned.1.call-start = ((), (), s32[]{:S(2)}) async-start(), calls=%async_computation.2 | async-start | bytes 6488064 | tf_op jit(solution)/shard_map/while/body/eval_jaxpr/all_gather | solution.py:48
  324.4 5.4 %slice-start = ((s8[6291456]{0:T(1024)(128)(4,1)}), s8[2097152]{0:T(1024)(128)(4,1)S(1)}, s32[]{:S(2)}) async-start(s8[6291456]{0:T(1024)(128)(4,1)} %bitcast.42), calls=%async_computation.3 | async-start | bytes 4194304 | tf_op jit(solution)/shard_map/while
  324.4 5.4 %slice-start.1 = ((s8[6291456]{0:T(1024)(128)(4,1)}), s8[4194304]{0:T(1024)(128)(4,1)S(1)}, s32[]{:S(2)}) async-start(s8[6291456]{0:T(1024)(128)(4,1)} %bitcast.42), calls=%async_computation.4 | async-start | bytes 8388608 | tf_op jit(solution)/shard_map/while
  324.4 5.8 %copy-start.5 = (bf16[2,2048,256]{2,1,0:T(8,128)(2,1)S(1)}, bf16[2,2048,256]{2,1,0:T(8,128)(2,1)}, u32[]{:S(2)}) copy-start(bf16[2,2048,256]{2,1,0:T(8,128)(2,1)} %get-tuple-element.376) | copy-start | bytes 6291460 | tf_op jit(solution)/shard_map/while
  330.2 2.9 copy-start.4
  424.1 10.9 %slice-start.2 = ((s8[6291456]{0:T(1024)(128)(4,1)}), s8[2097152]{0:T(1024)(128)(4,1)S(1)}, s32[]{:S(2)}) async-start(s8[6291456]{0:T(1024)(128)(4,1)} %bitcast.44), calls=%async_computation.5 | async-start | bytes 4194304
  429.6 5.4 %slice-start.3 = ((s8[6291456]{0:T(1024)(128)(4,1)}), s8[4194304]{0:T(1024)(128)(4,1)S(1)}, s32[]{:S(2)}) async-start(s8[6291456]{0:T(1024)(128)(4,1)} %bitcast.44), calls=%async_computation.6 | async-start | bytes 8388608
  429.6 5.9 %copy-start.1 = (f32[2,2048,256]{2,1,0:T(8,128)S(1)}, f32[2,2048,256]{2,1,0:T(8,128)}, u32[]{:S(2)}) copy-start(f32[2,2048,256]{2,1,0:T(8,128)} %copy.13) | copy-start | bytes 12582916
  435.5 6.7 %copy-start.2 = (f32[2,768,256]{2,1,0:T(8,128)}, f32[2,768,256]{2,1,0:T(8,128)S(1)}, u32[]{:S(2)}) copy-start(f32[2,768,256]{2,1,0:T(8,128)S(1)} %fusion.36) | copy-start | bytes 4718596
  435.5 6.7 %copy-start.6 = (bf16[2,2048,256]{2,1,0:T(8,128)(2,1)S(1)}, bf16[2,2048,256]{2,1,0:T(8,128)(2,1)}, u32[]{:S(2)}) copy-start(bf16[2,2048,256]{2,1,0:T(8,128)(2,1)} %get-tuple-element.393) | copy-start | bytes 6291460
  445.6 5.5 %copy-start.3 = (f32[2,768,256]{2,1,0:T(8,128)S(1)}, f32[2,768,256]{2,1,0:T(8,128)}, u32[]{:S(2)}) copy-start(f32[2,768,256]{2,1,0:T(8,128)} %copy-done.2) | copy-start | bytes 4718596
Sparse Core Ops, SparseCore 0:
  26.0 94.3 all-gather.7
  126.2 90.1 all-gather.9
  226.9 90.1 all-gather.9
  327.3 90.1 all-gather.9
where the time goes:
time: 468 us; the launch traced here: 467 us
  waiting for transfers between devices  314 us (67%)
  matrix products  84.4 us (18%)
  local copies, waits for them, and re-layouts  37.3 us (8%)
  blocking collectives  15.1 us (3%)
  between operations  13.8 us (3%)
    all_gather x4, waiting for transfers between devices, gather(): return lax.all_gather(piece, 'fsdp', axis=1, tiled=True)  314 us
    dot_general x4, matrix products, chunk_pass(): jnp.einsum('grd,grf->gdf', rows, gate_delta, preferred_element_type=jnp.f...  27.2 us
    dot_general x4, matrix products, chunk_pass(): jnp.einsum('grd,grf->gdf', rows, up_delta, preferred_element_type=jnp.flo...  23.4 us
    dot_general x4, matrix products, chunk_pass(): jnp.einsum('grd,gdf->grf', rows, gate_w, preferred_element_type=jnp.float32)  21.4 us
    while x27, local copies, waits for them, and re-layouts  21 us
    all_to_all x1, blocking collectives, on_device(): lax.all_to_all(outgoing, 'expert', split_axis=0, concat_axis=0, tiled=True)  15.1 us
    dot_general x4, matrix products, chunk_pass(): jnp.einsum('grd,gdf->grf', rows, up_w, preferred_element_type=jnp.float32)  12.2 us
    while x2, local copies, waits for them, and re-layouts, on_device(): lax.fori_loop(0, owners - 1, body, (rows, hidden_buf, gate_acc, up_acc))  11 us
  transfers between devices with their start and end apart: 4, of which 4 were waited for; matrix products, arithmetic and copies ran while one was open for 13% of the time, Pallas kernels for 0%

commit v1 on v0

--- a/solution.py
+++ b/solution.py
@@ -4,6 +4,13 @@
 from jax.sharding import PartitionSpec as P
 
 CAP = 24
+
+
+def all_by_exchange(array, mesh_axis, dim):
+    size = lax.axis_size(mesh_axis)
+    blocks = jnp.stack([array for _ in range(size)])
+    blocks = lax.all_to_all(blocks, mesh_axis, split_axis=0, concat_axis=0)
+    return jnp.concatenate(blocks, axis=dim)
 
 
 def chunk_pass(rows, gate_w, up_w, cotan):
@@ -45,7 +52,7 @@
 
     def gather(source):
         piece = lax.dynamic_index_in_dim(arrived, source, axis=0, keepdims=False)
-        return lax.all_gather(piece, "fsdp", axis=1, tiled=True)
+        return all_by_exchange(piece, "fsdp", 1)
 
     def step(source, rows, hidden_buf, gate_acc, up_acc):
         start = source * slot_count

time: 468 us -> 471 us (level)
  the two profiles are of different devices: /device:TPU:1 before, /device:TPU:4 now
where the time goes in v1:
time: 471 us; the launch traced here: 470 us
  waiting for transfers between devices  279 us (59%)
  matrix products  91.9 us (20%)
  local copies, waits for them, and re-layouts  54.2 us (12%)
  starting transfers between devices  27.5 us (6%)
  blocking collectives  14.6 us (3%)
    all_to_all x4, waiting for transfers between devices, all_by_exchange(): blocks = lax.all_to_all(blocks, mesh_axis, split_axis=0, concat_axis=0)  279 us
    dot_general x4, matrix products, chunk_pass(): jnp.einsum('grd,grf->gdf', rows, gate_delta, preferred_element_type=jnp.f...  27.5 us
    all_to_all x4, starting transfers between devices, all_by_exchange(): blocks = lax.all_to_all(blocks, mesh_axis, split_axis=0, concat_axis=0)  27.5 us
    all_to_all x4, local copies, waits for them, and re-layouts, all_by_exchange(): blocks = lax.all_to_all(blocks, mesh_axis, split_axis=0, concat_axis=0)  26.3 us
    dot_general x4, matrix products, chunk_pass(): jnp.einsum('grd,grf->gdf', rows, up_delta, preferred_element_type=jnp.flo...  23.6 us
    dot_general x4, matrix products, chunk_pass(): jnp.einsum('grd,gdf->grf', rows, up_w, preferred_element_type=jnp.float32)  20.9 us
    dot_general x4, matrix products, chunk_pass(): jnp.einsum('grd,gdf->grf', rows, gate_w, preferred_element_type=jnp.float32)  19.5 us
    all_to_all x1, blocking collectives, on_device(): lax.all_to_all(outgoing, 'expert', split_axis=0, concat_axis=0, tiled=True)  14.6 us
  transfers between devices with their start and end apart: 4, of which 4 were waited for; matrix products, arithmetic and copies ran while one was open for 14% of the time, Pallas kernels for 0%

profile of v1, /device:TPU:4, one launch (start us, length us, event | category | flops | bytes accessed | tf_op | source)
XLA Modules:
  0.0 470.5 jit_solution(4766998902174002769)
XLA Ops:
  3.5 14.6 %all_to_all.24 = bf16[4,2,24,2048]{3,2,1,0:T(8,128)(2,1)S(1)} all-to-all(bf16[4,2,24,2048]{3,2,1,0:T(8,128)(2,1)S(1)} %bitcast.56), channel_id=1, replica_groups=mesh['expert'=4,'fsdp'=32] {'expert'}, dimensions={0} | all-to-all | bytes 1572864 | tf_op jit(solution)/shard_map/all_to_all | solution.py:50
  18.2 3.5 stack.6
  21.6 10.7 %all-to-all-start.2 = ((bf16[32,2,24,2048]{3,2,1,0:T(8,128)(2,1)}), bf16[32,2,24,2048]{3,2,1,0:T(8,128)(2,1)}, u32[]{:S(2)}, u32[]{:S(2)}) async-start(bf16[32,2,24,2048]{3,2,1,0:T(8,128)(2,1)} %stack.6), calls=%async_computation.2 | async-start | bytes 12582912 | tf_op jit(solution)/shard_map/all_to_all | solution.py:12
  32.3 88.0 %all-to-all-done.2 = bf16[32,2,24,2048]{3,2,1,0:T(8,128)(2,1)} async-done(((bf16[32,2,24,2048]{3,2,1,0:T(8,128)(2,1)}), bf16[32,2,24,2048]{3,2,1,0:T(8,128)(2,1)}, u32[]{:S(2)}, u32[]{:S(2)}) %all-to-all-start.2) | async-done | bytes 6291488 | tf_op jit(solution)/shard_map/all_to_all | solution.py:12
  120.3 6.6 %copy.23 = bf16[32,2,24,2048]{3,2,0,1:T(8,128)(2,1)} copy(bf16[32,2,24,2048]{3,2,1,0:T(8,128)(2,1)} %all-to-all-done.2) | data formatting | bytes 12582912 | tf_op jit(solution)/shard_map/all_to_all | solution.py:12
  129.5 304.3 %while.22 = (s32[]{:T(128)}, bf16[2,768,2048]{2,1,0:T(8,128)(2,1)}, bf16[2,3072,256]{2,1,0:T(8,128)(2,1)}, f32[2,2048,256]{1,2,0:T(8,128)}, f32[2,2048,256]{1,2,...) while((s32[]{:T(128)}, bf16[2,768,2048]{2,1,0:T(8,128)(2,1)}, ...), condition=%wide.region_3.4_spmd.clone, body=%wide.region_2.3_spmd.clone.sunk | while | flops 6456082432 | bytes 136118656 | solution.py:74
  132.9 5.0 %all-to-all-start = ((bf16[32,2,24,2048]{3,2,1,0:T(8,128)(2,1)}), bf16[32,2,24,2048]{3,2,1,0:T(8,128)(2,1)}, u32[]{:S(2)}, u32[]{:S(2)}) async-start(bf16[32,2,24,2048]{3,2,1,0:T(8,128)(2,1)} %stack.9), calls=%async_computation | async-start | bytes 12582912 | tf_op jit(solution)/shard_map/while/body/eval_jaxpr/all_to_all | solution.py:12
  137.9 4.7 %fusion.68 = f32[2,768,256]{2,1,0:T(8,128)S(1)} fusion(bf16[2,768,2048]{2,1,0:T(8,128)(2,1)} %get-tuple-element.356, bf16[2,2048,256]{2,1,0:T(8,128)(2,1)S(1)} %get-tuple-element.375), kind=kOutput, calls=%fused_computation.52.clone.1 | convolution fusion | flops 1610612736 | bytes 9961472 | tf_op jit(solution)/shard_map/while/body/eval_jaxpr/grd,gdf->grf/dot_general | solution.py:17
  142.7 5.8 %fusion.69 = (bf16[2,3072,256]{2,1,0:T(8,128)(2,1)}, f32[2,768,256]{2,1,0:T(8,128)S(1)}) fusion(bf16[2,3072,256]{2,1,0:T(8,128)(2,1)} %get-tuple-element.357, s32[]{:T(128)S(6)} %select_n.61, f32[2,768,256]{2,1,0:T(8,128)S(1)} %fusion.68, bf16[2,768,2048]{2,1,0:T(8,128)(2,1)} %get-tuple-element.356, bf16[2,2048,256]{2,1,0:T(8,128)(2,1)S(1)} %copy-done.7), kind=kOutput, calls=%fused_computation.11.clone.1 | convolution fusion | flops 1612972032 | bytes 12320772 | tf_op jit(solution)/shard_map/while/body/eval_jaxpr/grd,gdf->grf/dot_general | solution.py:18
  148.6 4.2 bitcast_add_fusion.5
  152.7 4.5 bitcast_add_fusion.4
  157.2 65.6 %all-to-all-done = bf16[32,2,24,2048]{3,2,1,0:T(8,128)(2,1)} async-done(((bf16[32,2,24,2048]{3,2,1,0:T(8,128)(2,1)}), bf16[32,2,24,2048]{3,2,1,0:T(8,128)(2,1)}, u32[]{:S(2)}, u32[]{:S(2)}) %all-to-all-start) | async-done | bytes 6291488 | tf_op jit(solution)/shard_map/while/body/eval_jaxpr/all_to_all | solution.py:12
  222.8 6.6 %copy.33 = bf16[32,2,24,2048]{3,2,0,1:T(8,128)(2,1)} copy(bf16[32,2,24,2048]{3,2,1,0:T(8,128)(2,1)} %all-to-all-done) | data formatting | bytes 12582912 | tf_op jit(solution)/shard_map/while/body/eval_jaxpr/all_to_all | solution.py:12
  232.8 5.9 %all-to-all-start = ((bf16[32,2,24,2048]{3,2,1,0:T(8,128)(2,1)}), bf16[32,2,24,2048]{3,2,1,0:T(8,128)(2,1)}, u32[]{:S(2)}, u32[]{:S(2)}) async-start(bf16[32,2,24,2048]{3,2,1,0:T(8,128)(2,1)} %stack.9), calls=%async_computation | async-start | bytes 12582912 | tf_op jit(solution)/shard_map/while/body/eval_jaxpr/all_to_all | solution.py:12
  238.7 4.7 %fusion.68 = f32[2,768,256]{2,1,0:T(8,128)S(1)} fusion(bf16[2,768,2048]{2,1,0:T(8,128)(2,1)} %get-tuple-element.356, bf16[2,2048,256]{2,1,0:T(8,128)(2,1)S(1)} %get-tuple-element.375), kind=kOutput, calls=%fused_computation.52.clone.1 | convolution fusion | flops 1610612736 | bytes 9961472 | tf_op jit(solution)/shard_map/while/body/eval_jaxpr/grd,gdf->grf/dot_general | solution.py:17
  243.4 5.8 %fusion.69 = (bf16[2,3072,256]{2,1,0:T(8,128)(2,1)}, f32[2,768,256]{2,1,0:T(8,128)S(1)}) fusion(bf16[2,3072,256]{2,1,0:T(8,128)(2,1)} %get-tuple-element.357, s32[]{:T(128)S(6)} %select_n.61, f32[2,768,256]{2,1,0:T(8,128)S(1)} %fusion.68, bf16[2,768,2048]{2,1,0:T(8,128)(2,1)} %get-tuple-element.356, bf16[2,2048,256]{2,1,0:T(8,128)(2,1)S(1)} %copy-done.7), kind=kOutput, calls=%fused_computation.11.clone.1 | convolution fusion | flops 1612972032 | bytes 12320772 | tf_op jit(solution)/shard_map/while/body/eval_jaxpr/grd,gdf->grf/dot_general | solution.py:18
  249.3 6.4 %bitcast_add_fusion.5 = f32[2,2048,256]{1,2,0:T(8,128)} fusion(f32[2,2048,256]{1,2,0:T(8,128)} %get-tuple-element.359, bf16[2,768,2048]{2,1,0:T(8,128)(2,1)S(1)} %bitcast.52, pred[]{:T(512)S(6)} %compare.14, bf16[2,3072,256]{2,1,0:T(8,128)(2,1)S(1)} %copy-done.5, s32[]{:T(128)S(6)} %select_n.61, f32[2,768,256]{2,1,0:T(8,128)S(1)} %fusion.68), kind=kOutput, calls=%fused_computation.clone.1 | convolution fusion | flops 1615462400 | bytes 17039364 | tf_op jit(solution)/shard_map/while/body/eval_jaxpr/grd,grf->gdf/dot_general | solution.py:26
  255.7 6.7 %bitcast_add_fusion.4 = f32[2,2048,256]{1,2,0:T(8,128)} fusion(f32[2,2048,256]{1,2,0:T(8,128)} %get-tuple-element.358, bf16[2,768,2048]{2,1,0:T(8,128)(2,1)S(1)} %bitcast.52, pred[]{:T(512)S(6)} %compare.14, f32[2,768,256]{2,1,0:T(8,128)S(1)} %get-tuple-element.340, f32[2,768,256]{2,1,0:T(8,128)S(1)} %fusion.68, ...), kind=kOutput, calls=%fused_computation.1.clone.1 | convolution fusion | flops 1617035264 | bytes 18612228 | tf_op jit(solution)/shard_map/while/body/eval_jaxpr/grd,grf->gdf/dot_general | solution.py:25
  262.3 62.1 %all-to-all-done = bf16[32,2,24,2048]{3,2,1,0:T(8,128)(2,1)} async-done(((bf16[32,2,24,2048]{3,2,1,0:T(8,128)(2,1)}), bf16[32,2,24,2048]{3,2,1,0:T(8,128)(2,1)}, u32[]{:S(2)}, u32[]{:S(2)}) %all-to-all-start) | async-done | bytes 6291488 | tf_op jit(solution)/shard_map/while/body/eval_jaxpr/all_to_all | solution.py:12
  324.4 6.6 %copy.33 = bf16[32,2,24,2048]{3,2,0,1:T(8,128)(2,1)} copy(bf16[32,2,24,2048]{3,2,1,0:T(8,128)(2,1)} %all-to-all-done) | data formatting | bytes 12582912 | tf_op jit(solution)/shard_map/while/body/eval_jaxpr/all_to_all | solution.py:12
  334.4 5.9 %all-to-all-start = ((bf16[32,2,24,2048]{3,2,1,0:T(8,128)(2,1)}), bf16[32,2,24,2048]{3,2,1,0:T(8,128)(2,1)}, u32[]{:S(2)}, u32[]{:S(2)}) async-start(bf16[32,2,24,2048]{3,2,1,0:T(8,128)(2,1)} %stack.9), calls=%async_computation | async-start | bytes 12582912 | tf_op jit(solution)/shard_map/while/body/eval_jaxpr/all_to_all | solution.py:12
  340.4 4.7 %fusion.68 = f32[2,768,256]{2,1,0:T(8,128)S(1)} fusion(bf16[2,768,2048]{2,1,0:T(8,128)(2,1)} %get-tuple-element.356, bf16[2,2048,256]{2,1,0:T(8,128)(2,1)S(1)} %get-tuple-element.375), kind=kOutput, calls=%fused_computation.52.clone.1 | convolution fusion | flops 1610612736 | bytes 9961472 | tf_op jit(solution)/shard_map/while/body/eval_jaxpr/grd,gdf->grf/dot_general | solution.py:17
  345.1 5.8 %fusion.69 = (bf16[2,3072,256]{2,1,0:T(8,128)(2,1)}, f32[2,768,256]{2,1,0:T(8,128)S(1)}) fusion(bf16[2,3072,256]{2,1,0:T(8,128)(2,1)} %get-tuple-element.357, s32[]{:T(128)S(6)} %select_n.61, f32[2,768,256]{2,1,0:T(8,128)S(1)} %fusion.68, bf16[2,768,2048]{2,1,0:T(8,128)(2,1)} %get-tuple-element.356, bf16[2,2048,256]{2,1,0:T(8,128)(2,1)S(1)} %copy-done.7), kind=kOutput, calls=%fused_computation.11.clone.1 | convolution fusion | flops 1612972032 | bytes 12320772 | tf_op jit(solution)/shard_map/while/body/eval_jaxpr/grd,gdf->grf/dot_general | solution.py:18
  351.0 6.4 %bitcast_add_fusion.5 = f32[2,2048,256]{1,2,0:T(8,128)} fusion(f32[2,2048,256]{1,2,0:T(8,128)} %get-tuple-element.359, bf16[2,768,2048]{2,1,0:T(8,128)(2,1)S(1)} %bitcast.52, pred[]{:T(512)S(6)} %compare.14, bf16[2,3072,256]{2,1,0:T(8,128)(2,1)S(1)} %copy-done.5, s32[]{:T(128)S(6)} %select_n.61, f32[2,768,256]{2,1,0:T(8,128)S(1)} %fusion.68), kind=kOutput, calls=%fused_computation.clone.1 | convolution fusion | flops 1615462400 | bytes 17039364 | tf_op jit(solution)/shard_map/while/body/eval_jaxpr/grd,grf->gdf/dot_general | solution.py:26
  357.4 6.7 %bitcast_add_fusion.4 = f32[2,2048,256]{1,2,0:T(8,128)} fusion(f32[2,2048,256]{1,2,0:T(8,128)} %get-tuple-element.358, bf16[2,768,2048]{2,1,0:T(8,128)(2,1)S(1)} %bitcast.52, pred[]{:T(512)S(6)} %compare.14, f32[2,768,256]{2,1,0:T(8,128)S(1)} %get-tuple-element.340, f32[2,768,256]{2,1,0:T(8,128)S(1)} %fusion.68, ...), kind=kOutput, calls=%fused_computation.1.clone.1 | convolution fusion | flops 1617035264 | bytes 18612228 | tf_op jit(solution)/shard_map/while/body/eval_jaxpr/grd,grf->gdf/dot_general | solution.py:25
  364.0 63.1 %all-to-all-done = bf16[32,2,24,2048]{3,2,1,0:T(8,128)(2,1)} async-done(((bf16[32,2,24,2048]{3,2,1,0:T(8,128)(2,1)}), bf16[32,2,24,2048]{3,2,1,0:T(8,128)(2,1)}, u32[]{:S(2)}, u32[]{:S(2)}) %all-to-all-start) | async-done | bytes 6291488 | tf_op jit(solution)/shard_map/while/body/eval_jaxpr/all_to_all | solution.py:12
  427.2 6.6 %copy.33 = bf16[32,2,24,2048]{3,2,0,1:T(8,128)(2,1)} copy(bf16[32,2,24,2048]{3,2,1,0:T(8,128)(2,1)} %all-to-all-done) | data formatting | bytes 12582912 | tf_op jit(solution)/shard_map/while/body/eval_jaxpr/all_to_all | solution.py:12
  433.8 5.5 %copy.27 = f32[2,2048,256]{2,1,0:T(8,128)} copy(f32[2,2048,256]{1,2,0:T(8,128)} %get-tuple-element.229) | data formatting | bytes 8388608 | tf_op jit(solution)/shard_map/while | solution.py:74
  439.3 5.3 %fusion.36 = f32[2,768,256]{2,1,0:T(8,128)S(1)} fusion(bf16[2,768,2048]{2,1,0:T(8,128)(2,1)} %get-tuple-element.227, bf16[2,2048,256]{2,1,0:T(8,128)(2,1)} %param.9), kind=kOutput, calls=%fused_computation.53 | convolution fusion | flops 1610612736 | bytes 9961472 | tf_op jit(solution)/shard_map/grd,gdf->grf/dot_general | solution.py:17
  445.2 6.7 %convolution_add_fusion = f32[2,2048,256]{2,1,0:T(8,128)} fusion(f32[2,2048,256]{2,1,0:T(8,128)S(1)} %copy-done.2, bf16[2,768,2048]{2,1,0:T(8,128)(2,1)S(1)} %bitcast.55, bf16[2,3072,256]{2,1,0:T(8,128)(2,1)} %get-tuple-element.387, f32[2,768,256]{2,1,0:T(8,128)S(1)} %fusion.36), kind=kOutput, calls=%fused_computation.20 | convolution fusion | flops 1614413824 | bytes 17039360 | tf_op jit(solution)/shard_map/grd,grf->gdf/dot_general | solution.py:26
  455.3 5.5 %copy.25 = f32[2,2048,256]{2,1,0:T(8,128)} copy(f32[2,2048,256]{1,2,0:T(8,128)} %get-tuple-element.228) | data formatting | bytes 8388608 | tf_op jit(solution)/shard_map/while | solution.py:74
  460.8 9.7 %convolution_add_fusion.1 = f32[2,2048,256]{2,1,0:T(8,128)} fusion(f32[2,2048,256]{2,1,0:T(8,128)} %copy.25, bf16[2,768,2048]{2,1,0:T(8,128)(2,1)} %get-tuple-element.227, f32[2,768,256]{2,1,0:T(8,128)} %get-tuple-element.281, f32[2,768,256]{2,1,0:T(8,128)S(1)} %copy-done.4, bf16[2,3072,256]{2,1,0:T(8,128)(2,1)} %get-tuple-element.387), kind=kOutput, calls=%fused_computation.21 | convolution fusion | flops 1615986688 | bytes 18612224 | tf_op jit(solution)/shard_map/grd,grf->gdf/dot_general | solution.py:25
  (62 shorter events, 19.7 us)
Async XLA Ops:
  0.6 2.5 copy-start
  21.6 98.7 %all-to-all-start.2 = ((bf16[32,2,24,2048]{3,2,1,0:T(8,128)(2,1)}), bf16[32,2,24,2048]{3,2,1,0:T(8,128)(2,1)}, u32[]{:S(2)}, u32[]{:S(2)}) async-start(bf16[32,2,24,2048]{3,2,1,0:T(8,128)(2,1)} %stack.6), calls=%async_computation.2 | async-start | bytes 12582912 | tf_op jit(solution)/shard_map/all_to_all | solution.py:12
  126.9 2.6 copy-start.6
  132.9 89.9 %all-to-all-start = ((bf16[32,2,24,2048]{3,2,1,0:T(8,128)(2,1)}), bf16[32,2,24,2048]{3,2,1,0:T(8,128)(2,1)}, u32[]{:S(2)}, u32[]{:S(2)}) async-start(bf16[32,2,24,2048]{3,2,1,0:T(8,128)(2,1)} %stack.9), calls=%async_computation | async-start | bytes 12582912 | tf_op jit(solution)/shard_map/while/body/eval_jaxpr/all_to_all | solution.py:12
  137.9 4.8 %copy-start.7 = (bf16[2,2048,256]{2,1,0:T(8,128)(2,1)S(1)}, bf16[2,2048,256]{2,1,0:T(8,128)(2,1)}, u32[]{:S(2)}) copy-start(bf16[2,2048,256]{2,1,0:T(8,128)(2,1)} %get-tuple-element.376) | copy-start | bytes 6291460 | tf_op jit(solution)/shard_map/while
  137.9 10.6 %slice-start = ((s8[6291456]{0:T(1024)(128)(4,1)}), s8[4194304]{0:T(1024)(128)(4,1)S(1)}, s32[]{:S(2)}) async-start(s8[6291456]{0:T(1024)(128)(4,1)} %bitcast.51), calls=%async_computation.3 | async-start | bytes 8388608 | tf_op jit(solution)/shard_map/while
  142.7 5.9 %slice-start.1 = ((s8[6291456]{0:T(1024)(128)(4,1)}), s8[2097152]{0:T(1024)(128)(4,1)S(1)}, s32[]{:S(2)}) async-start(s8[6291456]{0:T(1024)(128)(4,1)} %bitcast.51), calls=%async_computation.4 | async-start | bytes 4194304 | tf_op jit(solution)/shard_map/while
  142.7 5.9 %copy-start.5 = (bf16[2,3072,256]{2,1,0:T(8,128)(2,1)S(1)}, bf16[2,3072,256]{2,1,0:T(8,128)(2,1)}, u32[]{:S(2)}) copy-start(bf16[2,3072,256]{2,1,0:T(8,128)(2,1)} %get-tuple-element.377) | copy-start | bytes 9437188 | tf_op jit(solution)/shard_map/while
  232.8 91.7 %all-to-all-start = ((bf16[32,2,24,2048]{3,2,1,0:T(8,128)(2,1)}), bf16[32,2,24,2048]{3,2,1,0:T(8,128)(2,1)}, u32[]{:S(2)}, u32[]{:S(2)}) async-start(bf16[32,2,24,2048]{3,2,1,0:T(8,128)(2,1)} %stack.9), calls=%async_computation | async-start | bytes 12582912 | tf_op jit(solution)/shard_map/while/body/eval_jaxpr/all_to_all | solution.py:12
  238.7 4.8 %copy-start.7 = (bf16[2,2048,256]{2,1,0:T(8,128)(2,1)S(1)}, bf16[2,2048,256]{2,1,0:T(8,128)(2,1)}, u32[]{:S(2)}) copy-start(bf16[2,2048,256]{2,1,0:T(8,128)(2,1)} %get-tuple-element.376) | copy-start | bytes 6291460 | tf_op jit(solution)/shard_map/while
  238.7 10.6 %slice-start = ((s8[6291456]{0:T(1024)(128)(4,1)}), s8[4194304]{0:T(1024)(128)(4,1)S(1)}, s32[]{:S(2)}) async-start(s8[6291456]{0:T(1024)(128)(4,1)} %bitcast.51), calls=%async_computation.3 | async-start | bytes 8388608 | tf_op jit(solution)/shard_map/while
  243.4 5.9 %slice-start.1 = ((s8[6291456]{0:T(1024)(128)(4,1)}), s8[2097152]{0:T(1024)(128)(4,1)S(1)}, s32[]{:S(2)}) async-start(s8[6291456]{0:T(1024)(128)(4,1)} %bitcast.51), calls=%async_computation.4 | async-start | bytes 4194304 | tf_op jit(solution)/shard_map/while
  243.4 5.9 %copy-start.5 = (bf16[2,3072,256]{2,1,0:T(8,128)(2,1)S(1)}, bf16[2,3072,256]{2,1,0:T(8,128)(2,1)}, u32[]{:S(2)}) copy-start(bf16[2,3072,256]{2,1,0:T(8,128)(2,1)} %get-tuple-element.377) | copy-start | bytes 9437188 | tf_op jit(solution)/shard_map/while
  334.4 92.8 %all-to-all-start = ((bf16[32,2,24,2048]{3,2,1,0:T(8,128)(2,1)}), bf16[32,2,24,2048]{3,2,1,0:T(8,128)(2,1)}, u32[]{:S(2)}, u32[]{:S(2)}) async-start(bf16[32,2,24,2048]{3,2,1,0:T(8,128)(2,1)} %stack.9), calls=%async_computation | async-start | bytes 12582912 | tf_op jit(solution)/shard_map/while/body/eval_jaxpr/all_to_all | solution.py:12
  340.4 4.8 %copy-start.7 = (bf16[2,2048,256]{2,1,0:T(8,128)(2,1)S(1)}, bf16[2,2048,256]{2,1,0:T(8,128)(2,1)}, u32[]{:S(2)}) copy-start(bf16[2,2048,256]{2,1,0:T(8,128)(2,1)} %get-tuple-element.376) | copy-start | bytes 6291460 | tf_op jit(solution)/shard_map/while
  340.4 10.6 %slice-start = ((s8[6291456]{0:T(1024)(128)(4,1)}), s8[4194304]{0:T(1024)(128)(4,1)S(1)}, s32[]{:S(2)}) async-start(s8[6291456]{0:T(1024)(128)(4,1)} %bitcast.51), calls=%async_computation.3 | async-start | bytes 8388608 | tf_op jit(solution)/shard_map/while
  345.1 5.9 %slice-start.1 = ((s8[6291456]{0:T(1024)(128)(4,1)}), s8[2097152]{0:T(1024)(128)(4,1)S(1)}, s32[]{:S(2)}) async-start(s8[6291456]{0:T(1024)(128)(4,1)} %bitcast.51), calls=%async_computation.4 | async-start | bytes 4194304 | tf_op jit(solution)/shard_map/while
  345.1 5.9 %copy-start.5 = (bf16[2,3072,256]{2,1,0:T(8,128)(2,1)S(1)}, bf16[2,3072,256]{2,1,0:T(8,128)(2,1)}, u32[]{:S(2)}) copy-start(bf16[2,3072,256]{2,1,0:T(8,128)(2,1)} %get-tuple-element.377) | copy-start | bytes 9437188 | tf_op jit(solution)/shard_map/while
  433.8 10.9 %slice-start.2 = ((s8[6291456]{0:T(1024)(128)(4,1)}), s8[2097152]{0:T(1024)(128)(4,1)S(1)}, s32[]{:S(2)}) async-start(s8[6291456]{0:T(1024)(128)(4,1)} %bitcast.54), calls=%async_computation.5 | async-start | bytes 4194304
  439.3 5.4 %slice-start.3 = ((s8[6291456]{0:T(1024)(128)(4,1)}), s8[4194304]{0:T(1024)(128)(4,1)S(1)}, s32[]{:S(2)}) async-start(s8[6291456]{0:T(1024)(128)(4,1)} %bitcast.54), calls=%async_computation.6 | async-start | bytes 8388608
  439.3 5.9 %copy-start.2 = (f32[2,2048,256]{2,1,0:T(8,128)S(1)}, f32[2,2048,256]{2,1,0:T(8,128)}, u32[]{:S(2)}) copy-start(f32[2,2048,256]{2,1,0:T(8,128)} %copy.27) | copy-start | bytes 12582916
  445.2 6.7 %copy-start.3 = (f32[2,768,256]{2,1,0:T(8,128)}, f32[2,768,256]{2,1,0:T(8,128)S(1)}, u32[]{:S(2)}) copy-start(f32[2,768,256]{2,1,0:T(8,128)S(1)} %fusion.36) | copy-start | bytes 4718596
  445.2 6.7 %copy-start.8 = (bf16[2,2048,256]{2,1,0:T(8,128)(2,1)S(1)}, bf16[2,2048,256]{2,1,0:T(8,128)(2,1)}, u32[]{:S(2)}) copy-start(bf16[2,2048,256]{2,1,0:T(8,128)(2,1)} %get-tuple-element.389) | copy-start | bytes 6291460
  455.3 5.5 %copy-start.4 = (f32[2,768,256]{2,1,0:T(8,128)S(1)}, f32[2,768,256]{2,1,0:T(8,128)}, u32[]{:S(2)}) copy-start(f32[2,768,256]{2,1,0:T(8,128)} %copy-done.3) | copy-start | bytes 4718596
  460.8 9.7 %copy-start.1 = (bf16[128,2048]{1,0:T(8,128)(2,1)S(1)}, bf16[128,2048]{1,0:T(8,128)(2,1)}, u32[]{:S(2)}) copy-start(bf16[128,2048]{1,0:T(8,128)(2,1)} %param.7) | copy-start | bytes 1572868
